TPU v7x, 256 devices: a whole 4x4x8 slice. The times are simulated.
256 devices in a mesh: dp: 32 (over x, z), own: 8 (over y, core).
Axes of the slice: x: 4, y: 4, z: 8, core: 2. Of those that a mesh axis runs over, the one named last changes fastest.
Arguments:
- partials: bfloat16 [32, 64, 256, 1024], P('dp', None, None, 'own')
- owner: int32 [64, 1], replicated, may hold values from 0 to 31; in each aligned block of 64 rows (0 to 63, 64 to 127, ...) at most 4 rows name the same one
- momentum: float32 [32, 4, 256, 1024], P('dp', None, None, 'own'), may hold values from -1.2 to 1.2
- master: float32 [32, 4, 256, 1024], P('dp', None, None, 'own'), may hold values from -0.3 to 0.3
Outputs:
- new_momentum: float32 [32, 4, 256, 1024], P('dp', None, None, 'own')
- new_master: float32 [32, 4, 256, 1024], P('dp', None, None, 'own')
- new_weights: bfloat16 [64, 256, 1024], P(None, None, 'own')
Inputs may be any that keep to these rules, and one draw needn't show every extreme that they name: `owner`: every group owns at least one block and at most 4 blocks; some group owns exactly 4.
All inputs are finite; a program needn't handle non-finite values.
Results may differ from a plain program's by a relative error of at most 0.0007.
Values may be sent and summed in bfloat16 or wider, within the bound.
No kernel may reach another device: no remote copies, remote signals or barrier semaphores. Data moves between devices by JAX's collectives and lax.ppermute only.
A program may use at most 128 MiB of HBM per device.

v0:
```python
import math
import jax
import jax.numpy as jnp
from jax import lax
from jax.sharding import PartitionSpec as P

D = 1024
ITERS = 5
COEF_A = 3.4445
COEF_B = -4.775
COEF_C = 2.0315
BETA = 0.95
STEP_SIZE = 0.2
DECAY = 0.1
EPSILON = 1e-07


def slot_targets(owner_list, group_count, slot_count):
    onehot = (owner_list[:, None] == jnp.arange(group_count, dtype=jnp.int32)[None, :]).astype(
        jnp.int32
    )
    before = jnp.cumsum(onehot, axis=0) - onehot
    ranks = jnp.sum(before * onehot, axis=1)
    return owner_list * slot_count + ranks


def slot_sources(target, slot_count, block_count):
    positions = jnp.arange(slot_count, dtype=jnp.int32)
    matches = positions[:, None] == target[None, :]
    present = jnp.any(matches, axis=1)
    source = jnp.sum(
        jnp.where(matches, jnp.arange(block_count, dtype=jnp.int32)[None, :], 0), axis=1
    )
    return (present, source)


def local_gram(values):
    return jnp.einsum(
        "srk,stk->srt",
        values,
        values,
        precision=lax.Precision.HIGHEST,
        preferred_element_type=jnp.float32,
    )


def gram_total(values):
    return lax.psum(local_gram(values), "own")


def newton_turn(ortho, gram):
    square = jnp.einsum(
        "srt,stu->sru",
        gram,
        gram,
        precision=lax.Precision.HIGHEST,
        preferred_element_type=jnp.float32,
    )
    poly = COEF_B * gram + COEF_C * square
    product = jnp.einsum(
        "srt,stk->srk",
        poly,
        ortho,
        precision=lax.Precision.HIGHEST,
        preferred_element_type=jnp.float32,
    )
    return COEF_A * ortho + product


def on_device(partials, owner, momentum, master):
    group_count = lax.axis_size("dp")
    local_rows = partials[0]
    block_count = local_rows.shape[0]
    slot_count = momentum.shape[1]
    block_rows = momentum.shape[2]
    owner_list = owner[:, 0]
    target = slot_targets(owner_list, group_count, slot_count)
    present, source = slot_sources(target, group_count * slot_count, block_count)
    outgoing = jnp.where(
        present[:, None, None], jnp.take(local_rows, source, axis=0).astype(jnp.float32), 0.0
    )
    gradient = lax.psum_scatter(outgoing, "dp", scatter_dimension=0, tiled=True)
    momentum_new = BETA * momentum[0] + gradient
    update = gradient + BETA * momentum_new
    squares = lax.psum(jnp.sum(update * update, axis=(1, 2)), "own")
    factor = 1.0 / (jnp.sqrt(squares) + EPSILON)
    ortho = update * factor[:, None, None]
    gram = gram_total(ortho)
    for iteration in range(ITERS):
        if iteration > 0:
            gram = gram_total(ortho)
        ortho = newton_turn(ortho, gram)
    step_factor = STEP_SIZE * 0.2 * math.sqrt(max(block_rows, D))
    master_new = master[0] * (1.0 - STEP_SIZE * DECAY) - step_factor * ortho
    weights_low = master_new.astype(jnp.bfloat16)
    every_slot = lax.all_gather(weights_low, "dp", axis=0, tiled=True)
    weights = jnp.take(every_slot, target, axis=0)
    return (momentum_new[None], master_new[None], weights)


def solution(mesh):
    in_specs = (
        P("dp", None, None, "own"),
        P(),
        P("dp", None, None, "own"),
        P("dp", None, None, "own"),
    )
    out_specs = (P("dp", None, None, "own"), P("dp", None, None, "own"), P(None, None, "own"))
    return jax.shard_map(
        on_device, mesh=mesh, in_specs=in_specs, out_specs=out_specs, check_vma=False
    )
```

profile of v0, /device:TPU:1, one launch (start us, length us, event | category | flops | bytes accessed | tf_op | source)
XLA Modules:
  0.0 780.1 jit_solution(16891098648073873890)
XLA Ops:
  7.2 0.0 reduce-scatter.2.cloned.1.call-start
  7.2 0.7 fusion.13
  7.9 0.1 reduce_window_sum.11
  8.0 0.8 select_reduce_fusion.1
  8.9 0.7 multiply_add_fusion.1
  9.5 0.1 select_reduce_fusion
  9.7 0.1 fusion.14
  9.8 8.6 %gather_fusion = bf16[128,256,128]{2,1,0:T(8,128)(2,1)} fusion(bf16[64,256,128]{2,1,0:T(8,128)(2,1)} %bitcast.64, s32[1024]{0:T(1024)S(1)} %pad_clamp_fusion.1), kind=kCustom, calls=%fused_computation | custom fusion | bytes 16777728 | tf_op jit(solution)/shard_map/jit(_take)/gather | solution.py:80
  18.4 13.4 %convert_select_fusion = f32[128,256,128]{2,1,0:T(8,128)} fusion(bf16[128,256,128]{2,1,0:T(8,128)(2,1)} %gather_fusion, pred[128]{0:T(512)(128)(4,1)S(1)} %compare_and_fusion, pred[128]{0:T(512)(128)(4,1)S(1)} %fusion.14), kind=kLoop, calls=%fused_computation.2 | loop fusion | flops 12582912 | bytes 25166080 | tf_op jit(solution)/shard_map/jit(_where)/select_n | solution.py:79
  31.7 0.0 copy-start
  31.7 0.0 reduce-scatter.2.cloned.1.call-update
  31.8 0.0 all-reduce.6.cloned.1.call-start
  31.8 245.8 %reduce-scatter.2.cloned.1.call-done = f32[4,256,128]{2,1,0:T(8,128)} async-done(((f32[128,256,128]{2,1,0:T(8,128)}), f32[4,256,128]{2,1,0:T(8,128)}) %reduce-scatter.2.cloned.1.call-update) | async-done | bytes 524304 | tf_op jit(solution)/shard_map/reduce_scatter | solution.py:82
  277.7 0.0 copy-done
  277.7 1.9 multiply_reduce_fusion
  279.6 17.0 %psum.42 = f32[4]{0:T(128)S(1)} all-reduce(f32[4]{0:T(128)S(1)} %get-tuple-element.5), channel_id=1, replica_groups=mesh['dp'=32,'own'=8] {'own'}, use_global_device_ids=true, to_apply=%region_6.7 | all-reduce | flops 4 | bytes 32 | tf_op jit(solution)/shard_map/psum | solution.py:85
  296.6 3.3 fusion.7
  299.9 0.0 all-reduce.6.cloned.1.call-update
  299.9 0.0 all-reduce.8.cloned.1.call-start
  300.0 61.9 %all-reduce.6.cloned.1.call-done = f32[4,256,256]{2,1,0:T(8,128)} async-done(((f32[4,256,256]{2,1,0:T(8,128)}), f32[4,256,256]{2,1,0:T(8,128)}) %all-reduce.6.cloned.1.call-update) | async-done | bytes 1048592 | tf_op jit(solution)/shard_map/psum | solution.py:48
  361.9 3.3 fusion.4
  365.2 2.4 convolution_add_fusion.4
  367.6 2.0 fusion.17
  369.5 0.0 all-reduce.8.cloned.1.call-update
  369.6 0.2 all-reduce.10.cloned.1.call-start
  369.8 67.1 %all-reduce.8.cloned.1.call-done = f32[4,256,256]{2,1,0:T(8,128)} async-done(((f32[4,256,256]{2,1,0:T(8,128)}), f32[4,256,256]{2,1,0:T(8,128)}) %all-reduce.8.cloned.1.call-update) | async-done | bytes 1048592 | tf_op jit(solution)/shard_map/psum | solution.py:48
  436.9 3.3 fusion.3
  440.2 1.1 convolution_add_fusion.3
  441.3 2.0 fusion.18
  443.3 0.0 all-reduce.10.cloned.1.call-update
  443.3 0.0 all-reduce.12.cloned.1.call-start
  443.4 67.3 %all-reduce.10.cloned.1.call-done = f32[4,256,256]{2,1,0:T(8,128)} async-done(((f32[4,256,256]{2,1,0:T(8,128)}), f32[4,256,256]{2,1,0:T(8,128)}) %all-reduce.10.cloned.1.call-update) | async-done | bytes 1048592 | tf_op jit(solution)/shard_map/psum | solution.py:48
  510.7 3.3 fusion.2
  514.0 0.0 copy-start.1
  514.0 1.1 convolution_add_fusion.2
  515.1 2.0 fusion.19
  517.0 0.0 copy-start.2
  517.0 0.0 all-reduce.12.cloned.1.call-update
  517.1 0.0 all-reduce.14.cloned.1.call-start
  517.1 67.3 %all-reduce.12.cloned.1.call-done = f32[4,256,256]{2,1,0:T(8,128)} async-done(((f32[4,256,256]{2,1,0:T(8,128)}), f32[4,256,256]{2,1,0:T(8,128)}) %all-reduce.12.cloned.1.call-update) | async-done | bytes 1048592 | tf_op jit(solution)/shard_map/psum | solution.py:48
  584.5 3.3 fusion.1
  587.8 1.1 convolution_add_fusion.1
  588.8 2.0 fusion.20
  590.8 0.0 all-reduce.14.cloned.1.call-update
  590.8 0.3 all-gather.2.cloned.1.call-start
  591.1 67.1 %all-reduce.14.cloned.1.call-done = f32[4,256,256]{2,1,0:T(8,128)} async-done(((f32[4,256,256]{2,1,0:T(8,128)}), f32[4,256,256]{2,1,0:T(8,128)}) %all-reduce.14.cloned.1.call-update) | async-done | bytes 1048592 | tf_op jit(solution)/shard_map/psum | solution.py:48
  658.2 3.3 fusion
  661.5 0.0 copy-done.1
  661.5 2.0 fusion.16
  663.5 0.0 all-gather.2.cloned.1.call-update
  663.5 0.0 copy-done.2
  663.6 98.5 %all-gather.2.cloned.1.call-done = bf16[128,256,128]{2,1,0:T(8,128)(2,1)} async-done(((bf16[4,256,128]{2,1,0:T(8,128)(2,1)}), bf16[128,256,128]{2,1,0:T(8,128)(2,1)}) %all-gather.2.cloned.1.call-update) | async-done | bytes 8388624 | tf_op jit(solution)/shard_map/all_gather | solution.py:96
  762.1 6.5 gather_fusion.1
  768.6 4.6 broadcast_select_fusion
  (6 shorter events, 0.0 us)
Async XLA Ops:
  7.2 270.5 %reduce-scatter.2.cloned.1.call-start = ((), (), s32[]{:S(2)}) async-start(), calls=%async_computation.1 | async-start | bytes 17301504 | tf_op jit(solution)/shard_map/reduce_scatter | solution.py:82
  31.7 245.9 %copy-start = (f32[1,4,256,128]{3,2,1,0:T(8,128)S(1)}, f32[1,4,256,128]{3,2,1,0:T(8,128)}, u32[]{:S(2)}) copy-start(f32[1,4,256,128]{3,2,1,0:T(8,128)} %param.6) | copy-start | bytes 1572868
  31.8 330.1 %all-reduce.6.cloned.1.call-start = ((), (), s32[]{:S(2)}) async-start(), calls=%async_computation.2 | async-start | bytes 2097152 | tf_op jit(solution)/shard_map/psum | solution.py:48
  299.9 137.0 %all-reduce.8.cloned.1.call-start = ((), (), s32[]{:S(2)}) async-start(), calls=%async_computation.3 | async-start | bytes 2097152 | tf_op jit(solution)/shard_map/psum | solution.py:48
  369.6 141.1 %all-reduce.10.cloned.1.call-start = ((), (), s32[]{:S(2)}) async-start(), calls=%async_computation.4 | async-start | bytes 2097152 | tf_op jit(solution)/shard_map/psum | solution.py:48
  443.3 141.2 %all-reduce.12.cloned.1.call-start = ((), (), s32[]{:S(2)}) async-start(), calls=%async_computation.5 | async-start | bytes 2097152 | tf_op jit(solution)/shard_map/psum | solution.py:48
  514.0 147.5 %copy-start.1 = (f32[1,4,256,128]{3,2,1,0:T(8,128)S(1)}, f32[1,4,256,128]{3,2,1,0:T(8,128)}, u32[]{:S(2)}) copy-start(f32[1,4,256,128]{3,2,1,0:T(8,128)} %param.7) | copy-start | bytes 1572868
  517.0 146.5 %copy-start.2 = (s32[64,1]{0,1:T(1,128)S(1)}, s32[64,1]{0,1:T(1,128)}, u32[]{:S(2)}) copy-start(s32[64,1]{0,1:T(1,128)} %param.5) | copy-start | bytes 772
  517.1 141.1 %all-reduce.14.cloned.1.call-start = ((), (), s32[]{:S(2)}) async-start(), calls=%async_computation.6 | async-start | bytes 2097152 | tf_op jit(solution)/shard_map/psum | solution.py:48
  590.8 171.3 %all-gather.2.cloned.1.call-start = ((), (), s32[]{:S(2)}) async-start(), calls=%async_computation.7 | async-start | bytes 8650752 | tf_op jit(solution)/shard_map/all_gather | solution.py:96
Sparse Core Ops, SparseCore 0:
  31.9 245.7 reduce-scatter.1
  300.1 61.7 all-reduce.5
  369.7 67.2 all-reduce.7
  443.4 67.2 all-reduce.9
  517.2 67.2 all-reduce.11
  590.9 67.2 all-reduce.13
  663.6 98.4 all-gather.1
where the time goes:
time: 780 us
  waiting for transfers between devices  675 us (87%)
  matrix products  35.2 us (5%)
  other arithmetic  22.5 us (3%)
  blocking collectives  17 us (2%)
  local copies, waits for them, and re-layouts  15.1 us (2%)
  between operations  14.3 us (2%)
    psum x5, waiting for transfers between devices, gram_total(): return lax.psum(local_gram(values), 'own')  331 us
    reduce_scatter x1, waiting for transfers between devices, on_device(): gradient = lax.psum_scatter(outgoing, 'dp', scatter_dimension=0, tiled=True)  246 us
    all_gather x1, waiting for transfers between devices, on_device(): every_slot = lax.all_gather(weights_low, 'dp', axis=0, tiled=True)  98.5 us
    psum x1, blocking collectives, on_device(): squares = lax.psum(jnp.sum(update * update, axis=(1, 2)), 'own')  17 us
    dot_general x5, matrix products, newton_turn(): jnp.einsum('srt,stu->sru', gram, gram, precision=lax.Precision.HIGHEST, p...  16.5 us
  transfers between devices with their start and end apart: 7, of which 7 were waited for; matrix products, arithmetic and copies ran while one was open for 0% of the time, Pallas kernels for 0%

commit v1 on v0

--- a/solution.py
+++ b/solution.py
@@ -45,7 +45,7 @@
 
 
 def gram_total(values):
-    return lax.psum(local_gram(values), "own")
+    return jnp.sum(lax.all_gather(local_gram(values), "own"), axis=0)
 
 
 def newton_turn(ortho, gram):

time: 780 us -> 716 us (0.918)
  waiting for transfers between devices: 675 us -> 601 us
  other arithmetic: 22.5 us -> 42.9 us
  matrix products: 35.2 us -> 23.8 us
    psum x5 -> x0, waiting for transfers between devices: 331 us -> none  [gram_total(): return lax.psum(local_gram(values), 'own')]
    all_gather x0 -> x5, waiting for transfers between devices: none -> 258 us  [gram_total(): return jnp.sum(lax.all_gather(local_gram(values), 'own'), axis=0)]
    reduce_sum x0 -> x5, other arithmetic: none -> 20.3 us  [gram_total(): return jnp.sum(lax.all_gather(local_gram(values), 'own'), axis=0)]
    dot_general x5, matrix products: 16.5 us -> 6.29 us  [newton_turn(): jnp.einsum('srt,stu->sru', gram, gram, precision=lax.Precision.HIGHEST, p...]
where the time goes in v1:
time: 716 us; the launch traced here: 715 us
  waiting for transfers between devices  601 us (84%)
  other arithmetic  42.9 us (6%)
  matrix products  23.8 us (3%)
  blocking collectives  17 us (2%)
  local copies, waits for them, and re-layouts  15.1 us (2%)
  between operations  14.3 us (2%)
    all_gather x5, waiting for transfers between devices, gram_total(): return jnp.sum(lax.all_gather(local_gram(values), 'own'), axis=0)  258 us
    reduce_scatter x1, waiting for transfers between devices, on_device(): gradient = lax.psum_scatter(outgoing, 'dp', scatter_dimension=0, tiled=True)  246 us
    all_gather x1, waiting for transfers between devices, on_device(): every_slot = lax.all_gather(weights_low, 'dp', axis=0, tiled=True)  97 us
    reduce_sum x5, other arithmetic, gram_total(): return jnp.sum(lax.all_gather(local_gram(values), 'own'), axis=0)  20.3 us
    psum x1, blocking collectives, on_device(): squares = lax.psum(jnp.sum(update * update, axis=(1, 2)), 'own')  17 us
  transfers between devices with their start and end apart: 7, of which 7 were waited for; matrix products, arithmetic and copies ran while one was open for 0% of the time, Pallas kernels for 0%

profile of v1, /device:TPU:1, one launch (start us, length us, event | category | flops | bytes accessed | tf_op | source)
XLA Modules:
  0.0 715.1 jit_solution(15275610720060932895)
XLA Ops:
  7.2 0.0 reduce-scatter.2.cloned.1.call-start
  7.2 0.7 fusion.13
  7.9 0.1 reduce_window_sum.11
  8.0 0.8 select_reduce_fusion.1
  8.9 0.7 multiply_add_fusion.1
  9.5 0.1 select_reduce_fusion
  9.7 0.1 fusion.14
  9.8 8.6 %gather_fusion = bf16[128,256,128]{2,1,0:T(8,128)(2,1)} fusion(bf16[64,256,128]{2,1,0:T(8,128)(2,1)} %bitcast.69, s32[1024]{0:T(1024)S(1)} %pad_clamp_fusion.1), kind=kCustom, calls=%fused_computation | custom fusion | bytes 16777728 | tf_op jit(solution)/shard_map/jit(_take)/gather | solution.py:80
  18.4 13.4 %convert_select_fusion = f32[128,256,128]{2,1,0:T(8,128)} fusion(bf16[128,256,128]{2,1,0:T(8,128)(2,1)} %gather_fusion, pred[128]{0:T(512)(128)(4,1)S(1)} %compare_and_fusion, pred[128]{0:T(512)(128)(4,1)S(1)} %fusion.14), kind=kLoop, calls=%fused_computation.2 | loop fusion | flops 12582912 | bytes 25166080 | tf_op jit(solution)/shard_map/jit(_where)/select_n | solution.py:79
  31.7 0.0 copy-start
  31.7 0.0 reduce-scatter.2.cloned.1.call-update
  31.8 0.0 all-gather.14.cloned.1.call-start
  31.8 245.8 %reduce-scatter.2.cloned.1.call-done = f32[4,256,128]{2,1,0:T(8,128)} async-done(((f32[128,256,128]{2,1,0:T(8,128)}), f32[4,256,128]{2,1,0:T(8,128)}) %reduce-scatter.2.cloned.1.call-update) | async-done | bytes 524304 | tf_op jit(solution)/shard_map/reduce_scatter | solution.py:82
  277.7 0.0 copy-done
  277.7 0.0 copy-start.1
  277.7 2.0 multiply_reduce_fusion
  279.7 17.0 %psum.7 = f32[4]{0:T(128)S(1)} all-reduce(f32[4]{0:T(128)S(1)} %get-tuple-element.5), channel_id=1, replica_groups=mesh['dp'=32,'own'=8] {'own'}, use_global_device_ids=true, to_apply=%region_6.7 | all-reduce | flops 4 | bytes 32 | tf_op jit(solution)/shard_map/psum | solution.py:85
  296.7 3.3 fusion.7
  300.0 0.0 all-gather.14.cloned.1.call-update
  300.0 0.2 all-gather.16.cloned.1.call-start
  300.2 48.6 %all-gather.14.cloned.1.call-done = f32[32,256,256]{2,1,0:T(8,128)} async-done(((f32[4,256,256]{2,1,0:T(8,128)}), f32[32,256,256]{2,1,0:T(8,128)}) %all-gather.14.cloned.1.call-update) | async-done | bytes 8388624 | tf_op jit(solution)/shard_map/all_gather | solution.py:48
  348.8 4.1 reduce_sum.80
  352.9 1.3 fusion.4
  354.2 0.0 copy-done.1
  354.2 1.2 convolution_add_fusion.4
  355.3 2.0 fusion.17
  357.3 0.0 all-gather.16.cloned.1.call-update
  357.3 0.0 all-gather.18.cloned.1.call-start
  357.4 52.5 %all-gather.16.cloned.1.call-done = f32[32,256,256]{2,1,0:T(8,128)} async-done(((f32[4,256,256]{2,1,0:T(8,128)}), f32[32,256,256]{2,1,0:T(8,128)}) %all-gather.16.cloned.1.call-update) | async-done | bytes 8388624 | tf_op jit(solution)/shard_map/all_gather | solution.py:48
  409.9 4.1 reduce_sum.81
  414.0 1.3 fusion.3
  415.2 1.1 convolution_add_fusion.3
  416.3 2.0 fusion.18
  418.3 0.0 all-gather.18.cloned.1.call-update
  418.3 0.3 all-gather.20.cloned.1.call-start
  418.6 52.3 %all-gather.18.cloned.1.call-done = f32[32,256,256]{2,1,0:T(8,128)} async-done(((f32[4,256,256]{2,1,0:T(8,128)}), f32[32,256,256]{2,1,0:T(8,128)}) %all-gather.18.cloned.1.call-update) | async-done | bytes 8388624 | tf_op jit(solution)/shard_map/all_gather | solution.py:48
  470.9 4.1 reduce_sum.82
  474.9 1.3 fusion.2
  476.2 1.1 convolution_add_fusion.2
  477.3 2.0 fusion.19
  479.2 0.0 all-gather.20.cloned.1.call-update
  479.3 0.0 all-gather.22.cloned.1.call-start
  479.3 52.5 %all-gather.20.cloned.1.call-done = f32[32,256,256]{2,1,0:T(8,128)} async-done(((f32[4,256,256]{2,1,0:T(8,128)}), f32[32,256,256]{2,1,0:T(8,128)}) %all-gather.20.cloned.1.call-update) | async-done | bytes 8388624 | tf_op jit(solution)/shard_map/all_gather | solution.py:48
  531.8 4.1 reduce_sum.83
  535.9 1.3 fusion.1
  537.2 1.1 convolution_add_fusion.1
  538.2 0.0 copy-start.2
  538.2 2.0 fusion.20
  540.2 0.0 copy-start.3
  540.2 0.0 all-gather.22.cloned.1.call-update
  540.2 0.3 all-gather.12.cloned.1.call-start
  540.6 52.3 %all-gather.22.cloned.1.call-done = f32[32,256,256]{2,1,0:T(8,128)} async-done(((f32[4,256,256]{2,1,0:T(8,128)}), f32[32,256,256]{2,1,0:T(8,128)}) %all-gather.22.cloned.1.call-update) | async-done | bytes 8388624 | tf_op jit(solution)/shard_map/all_gather | solution.py:48
  592.8 4.1 reduce_sum.84
  596.9 1.3 fusion
  598.1 0.0 copy-done.2
  598.2 2.0 fusion.16
  600.1 0.0 all-gather.12.cloned.1.call-update
  600.1 0.0 copy-done.3
  600.2 97.0 %all-gather.12.cloned.1.call-done = bf16[128,256,128]{2,1,0:T(8,128)(2,1)} async-done(((bf16[4,256,128]{2,1,0:T(8,128)(2,1)}), bf16[128,256,128]{2,1,0:T(8,128)(2,1)}) %all-gather.12.cloned.1.call-update) | async-done | bytes 8388624 | tf_op jit(solution)/shard_map/all_gather | solution.py:96
  697.2 6.5 gather_fusion.1
  703.6 4.6 broadcast_select_fusion
  (6 shorter events, 0.0 us)
Async XLA Ops:
  7.2 270.5 %reduce-scatter.2.cloned.1.call-start = ((), (), s32[]{:S(2)}) async-start(), calls=%async_computation.1 | async-start | bytes 17301504 | tf_op jit(solution)/shard_map/reduce_scatter | solution.py:82
  31.7 245.9 %copy-start = (f32[1,4,256,128]{3,2,1,0:T(8,128)S(1)}, f32[1,4,256,128]{3,2,1,0:T(8,128)}, u32[]{:S(2)}) copy-start(f32[1,4,256,128]{3,2,1,0:T(8,128)} %param.6) | copy-start | bytes 1572868
  31.8 317.1 %all-gather.14.cloned.1.call-start = ((), (), s32[]{:S(2)}) async-start(), calls=%async_computation.3 | async-start | bytes 9437184 | tf_op jit(solution)/shard_map/all_gather | solution.py:48
  277.7 76.5 %copy-start.1 = (f32[4,256,128]{2,1,0:T(8,128)S(1)}, f32[4,256,128]{2,1,0:T(8,128)}, u32[]{:S(2)}) copy-start(f32[4,256,128]{2,1,0:T(8,128)} %reduce-scatter.2.cloned.1.call-done) | copy-start | bytes 1572868
  300.0 109.9 %all-gather.16.cloned.1.call-start = ((), (), s32[]{:S(2)}) async-start(), calls=%async_computation.4 | async-start | bytes 9437184 | tf_op jit(solution)/shard_map/all_gather | solution.py:48
  357.3 113.5 %all-gather.18.cloned.1.call-start = ((), (), s32[]{:S(2)}) async-start(), calls=%async_computation.5 | async-start | bytes 9437184 | tf_op jit(solution)/shard_map/all_gather | solution.py:48
  418.3 113.5 %all-gather.20.cloned.1.call-start = ((), (), s32[]{:S(2)}) async-start(), calls=%async_computation.6 | async-start | bytes 9437184 | tf_op jit(solution)/shard_map/all_gather | solution.py:48
  479.3 113.6 %all-gather.22.cloned.1.call-start = ((), (), s32[]{:S(2)}) async-start(), calls=%async_computation.7 | async-start | bytes 9437184 | tf_op jit(solution)/shard_map/all_gather | solution.py:48
  538.2 59.9 %copy-start.2 = (f32[1,4,256,128]{3,2,1,0:T(8,128)S(1)}, f32[1,4,256,128]{3,2,1,0:T(8,128)}, u32[]{:S(2)}) copy-start(f32[1,4,256,128]{3,2,1,0:T(8,128)} %param.7) | copy-start | bytes 1572868
  540.2 59.9 %copy-start.3 = (s32[64,1]{0,1:T(1,128)S(1)}, s32[64,1]{0,1:T(1,128)}, u32[]{:S(2)}) copy-start(s32[64,1]{0,1:T(1,128)} %param.5) | copy-start | bytes 772
  540.2 156.9 %all-gather.12.cloned.1.call-start = ((), (), s32[]{:S(2)}) async-start(), calls=%async_computation.2 | async-start | bytes 8650752 | tf_op jit(solution)/shard_map/all_gather | solution.py:96
Sparse Core Ops, SparseCore 0:
  31.9 245.7 reduce-scatter.1
  300.1 48.6 all-gather.13
  357.4 52.4 all-gather.15
  418.4 52.4 all-gather.17
  479.4 52.4 all-gather.19
  540.4 52.4 all-gather.21
  600.3 96.8 all-gather.11
